TPU v7x, 256 devices: a whole 4x4x8 slice. The times are simulated.
256 devices in a mesh: req: 64 (over z, y_lo, x), tp: 4 (over y_hi, core).
Axes of the slice: x: 4, y: 4 (y_hi: 2, y_lo: 2; y = y_hi * 2 + y_lo), z: 8, core: 2. Of those that a mesh axis runs over, the one named last changes fastest.
Arguments:
- hidden: bfloat16 [32768, 4096], P(('req', 'tp')), may hold values from -6 to 6
- norm_gain: bfloat16 [4096], replicated, may hold values from 0.099609375 to 1.8984375
- w_qkv: bfloat16 [4096, 3072], P('req', 'tp'), may hold values from -0.09375 to 0.09375
- w_out: bfloat16 [2048, 4096], P('tp', 'req'), may hold values from -0.125 to 0.125
- lengths: int32 [256], replicated, may hold values from 1 to 3072, as said below
- deal: int32 [256], replicated, may hold values from 0 to 255, as said below
- pages: int32 [256, 24], P('req'), may hold values from 0 to 95, as said below
- pool: bfloat16 [6144, 128, 1024], P('req', None, 'tp'), may hold values from -360 to 360
Outputs:
- attn_out: bfloat16 [32768, 4096], P(('req', 'tp'))
- new_kv: bfloat16 [32768, 1024], P('req', 'tp')
Inputs may be any that keep to these rules, and one draw needn't show every extreme that they name: `lengths`: at least one request has exactly 3072 cached tokens. `deal`: a permutation of the requests. `pages`: the 4 rows of one req index together hold each page number of its pool block once.
All inputs are finite; a program needn't handle non-finite values.
Results may differ from a plain program's by a relative error of at most 0.01.
The roundings to bfloat16 on the way count: a program that leaves them out, or rounds other values in their place, can miss the bound.
Values may be sent and summed in bfloat16 or wider, within the bound.
No kernel may reach another device: no remote copies, remote signals or barrier semaphores. Data moves between devices by JAX's collectives and lax.ppermute only.
A program may use at most 128 MiB of HBM per device.

v0:
```python
import math
import jax
import jax.numpy as jnp
from jax import lax
from jax.sharding import PartitionSpec as P

HEAD = 128
QH = 16
KVH = 4
PAGE = 128
NEW = 128


def rotate(values, position):
    half = values.shape[-1] // 2
    freqs = 500000.0 ** (-(jnp.arange(half, dtype=jnp.float32) * 2.0 / values.shape[-1]))
    angles = position.astype(jnp.float32)[:, None] * freqs[None, :]
    target = (angles.shape[0],) + (1,) * (values.ndim - 2) + (half,)
    cosine = jnp.cos(angles).reshape(target)
    sine = jnp.sin(angles).reshape(target)
    former = values[..., :half]
    latter = values[..., half:]
    return jnp.concatenate([former * cosine - latter * sine, latter * cosine + former * sine], -1)


def fresh_scores_of(query_matrix, recent_key_rows, score_scale):
    scores = (
        jnp.einsum("esv,qv->seq", query_matrix, recent_key_rows, preferred_element_type=jnp.float32)
        * score_scale
    )
    count_new = query_matrix.shape[0]
    causal = jnp.arange(count_new)[:, None] >= jnp.arange(count_new)[None, :]
    return jnp.where(causal, scores, -jnp.inf)


def value_weighted_rows(weights, values, form):
    return jnp.einsum(
        form, weights.astype(jnp.bfloat16), values, preferred_element_type=jnp.float32
    )


def padded_attention(
    query_matrix, recent_key_rows, recent_value_rows, pool, page_row, length, score_scale
):
    cache = pool[page_row].reshape(-1, 2 * HEAD)
    span = cache.shape[0]
    cached_scores = (
        jnp.einsum("ngd,kd->gnk", query_matrix, cache[:, :HEAD], preferred_element_type=jnp.float32)
        * score_scale
    )
    cached_scores = jnp.where(jnp.arange(span, dtype=jnp.int32) < length, cached_scores, -jnp.inf)
    recent_score_rows = fresh_scores_of(query_matrix, recent_key_rows, score_scale)
    row_max = jnp.maximum(cached_scores.max(-1), recent_score_rows.max(-1))[..., None]
    cached_exp = jnp.exp(cached_scores - row_max)
    recent_exponent = jnp.exp(recent_score_rows - row_max)
    total = cached_exp.sum(-1) + recent_exponent.sum(-1)
    summed_total = value_weighted_rows(cached_exp, cache[:, HEAD:], "gnk,kd->gnd")
    summed_total = summed_total + value_weighted_rows(
        recent_exponent, recent_value_rows, "vqa,as->vqs"
    )
    return summed_total / total[..., None]


REQ_AXES = ("z", "ylo", "x")
TP_AXES = ("yhi", "core")


def staged_gather(values, axes, axis):
    for name in reversed(axes):
        values = lax.all_gather(values, name, axis=axis, tiled=True)
    return values


def per_device(hidden, norm_gain, w_qkv, w_out, lengths, deal, pages, pool):
    states = hidden.astype(jnp.float32)
    mean_square = jnp.mean(states * states, axis=1, keepdims=True)
    normed = (states * lax.rsqrt(mean_square + 1e-05) * norm_gain.astype(jnp.float32)).astype(
        jnp.bfloat16
    )
    gathered = lax.all_gather(
        lax.all_gather(normed, "core", axis=0, tiled=True), "yhi", axis=0, tiled=True
    )
    tok_rows = gathered.shape[0]
    projected = jnp.dot(
        gathered, staged_gather(w_qkv, REQ_AXES, 0), preferred_element_type=jnp.float32
    ).astype(jnp.bfloat16)
    full_out = staged_gather(w_out, REQ_AXES, 1)
    group = QH // KVH
    heads_here = w_qkv.shape[1] // ((group + 2) * HEAD)
    assert heads_here == 1 and pool.shape[2] == 2 * HEAD
    slot_count = tok_rows // NEW
    slot_ids = lax.axis_index(REQ_AXES) * slot_count + jnp.arange(slot_count, dtype=jnp.int32)
    slot_length = lengths[deal[slot_ids]]
    position = jnp.repeat(slot_length, NEW) + jnp.tile(jnp.arange(NEW, dtype=jnp.int32), slot_count)
    projected = projected.reshape(tok_rows, group + 2, HEAD)
    queries = rotate(projected[:, :group].astype(jnp.float32), position).astype(jnp.bfloat16)
    keys_new = rotate(projected[:, group].astype(jnp.float32), position).astype(jnp.bfloat16)
    values_new = projected[:, group + 1]
    new_kv = jnp.concatenate([keys_new, values_new], 1)
    score_scale = 1.0 / math.sqrt(HEAD)

    def attend(local_slot):
        begin = local_slot * NEW
        query_matrix = lax.dynamic_slice_in_dim(queries, begin, NEW, 0)
        recent_key_rows = lax.dynamic_slice_in_dim(keys_new, begin, NEW, 0)
        recent_value_rows = lax.dynamic_slice_in_dim(values_new, begin, NEW, 0)
        page_row = pages[local_slot]
        length = slot_length[local_slot]
        result = padded_attention(
            query_matrix, recent_key_rows, recent_value_rows, pool, page_row, length, score_scale
        )
        result = result.astype(jnp.bfloat16)
        return result.transpose(1, 0, 2).reshape(NEW, group * HEAD)

    n_hi = lax.axis_size("yhi")
    n_core = lax.axis_size("core")
    order = jnp.arange(slot_count, dtype=jnp.int32)
    order = order % n_hi * n_core + order // n_hi
    contexts = lax.map(attend, order)
    context = contexts.reshape(tok_rows, group * HEAD)
    partial = jnp.dot(context, full_out, preferred_element_type=jnp.float32).astype(jnp.bfloat16)
    partial = lax.psum_scatter(partial, "core", scatter_dimension=0, tiled=True)
    attn_out = lax.psum_scatter(partial, "yhi", scatter_dimension=0, tiled=True)
    return (attn_out, new_kv)


def solution(mesh):
    fine = jax.sharding.Mesh(mesh.devices.reshape(8, 2, 4, 2, 2), REQ_AXES + TP_AXES)
    in_specs = (
        P(REQ_AXES + TP_AXES, None),
        P(),
        P(REQ_AXES, TP_AXES),
        P(TP_AXES, REQ_AXES),
        P(),
        P(),
        P(REQ_AXES, None),
        P(REQ_AXES, None, TP_AXES),
    )
    out_specs = (P(REQ_AXES + TP_AXES, None), P(REQ_AXES, TP_AXES))
    return jax.shard_map(
        per_device, mesh=fine, in_specs=in_specs, out_specs=out_specs, check_vma=False
    )
```

profile of v0, /device:TPU:1, one launch (start us, length us, event | category | flops | bytes accessed | tf_op | source)
XLA Modules:
  0.0 318.4 jit_solution(1034043087824753205)
XLA Ops:
  7.2 0.7 convert_element_type.48
  7.9 1.5 fusion.29
  9.5 2.5 fusion.31
  12.1 20.5 %all-gather.5.cloned.1.call-done = bf16[256,4096]{1,0:T(8,128)(2,1)} async-done(((bf16[128,4096]{1,0:T(8,128)(2,1)}), bf16[256,4096]{1,0:T(8,128)(2,1)}) %all-gather.5.cloned.1.call-update) | async-done | bytes 2097168 | tf_op jit(solution)/shard_map/all_gather | solution.py:81
  32.7 10.3 %all_gather.26 = bf16[256,768]{1,0:T(8,128)(2,1)S(1)} all-gather(bf16[64,768]{1,0:T(8,128)(2,1)S(1)} %copy-done.2), channel_id=1, replica_groups=mesh['z'=8,'ylo'=2,'x'=4,'yhi'=2,'core'=2] {'x'}, dimensions={0}, use_global_device_ids=true | all-gather | bytes 491520 | tf_op jit(solution)/shard_map/all_gather | solution.py:70
  43.0 8.9 %all_gather.27 = bf16[512,768]{1,0:T(8,128)(2,1)} all-gather(bf16[256,768]{1,0:T(8,128)(2,1)S(1)} %all_gather.26), channel_id=1, replica_groups=mesh['z'=8,'ylo'=2,'x'=4,'yhi'=2,'core'=2] {'ylo'}, dimensions={0}, use_global_device_ids=true | all-gather | bytes 1179648 | tf_op jit(solution)/shard_map/all_gather | solution.py:70
  52.0 10.6 %all_gather.29 = bf16[512,256]{0,1:T(8,128)(2,1)S(1)} all-gather(bf16[512,64]{0,1:T(8,128)(2,1)S(1)} %copy-done.3), channel_id=1, replica_groups=mesh['z'=8,'ylo'=2,'x'=4,'yhi'=2,'core'=2] {'x'}, dimensions={1}, use_global_device_ids=true | all-gather | bytes 327680 | tf_op jit(solution)/shard_map/all_gather | solution.py:70
  62.6 12.4 %all_gather.30 = bf16[512,512]{0,1:T(8,128)(2,1)} all-gather(bf16[512,256]{0,1:T(8,128)(2,1)S(1)} %all_gather.29), channel_id=1, replica_groups=mesh['z'=8,'ylo'=2,'x'=4,'yhi'=2,'core'=2] {'ylo'}, dimensions={1}, use_global_device_ids=true | all-gather | bytes 786432 | tf_op jit(solution)/shard_map/all_gather | solution.py:70
  75.1 0.6 gather_fusion.1
  75.8 0.6 gather_fusion.2
  76.5 31.1 %all-gather.7.cloned.1.call-done = bf16[512,4096]{1,0:T(8,128)(2,1)} async-done(((bf16[256,4096]{1,0:T(8,128)(2,1)}), bf16[512,4096]{1,0:T(8,128)(2,1)}) %all-gather.7.cloned.1.call-update) | async-done | bytes 4194320 | tf_op jit(solution)/shard_map/all_gather | solution.py:80
  107.6 73.8 %all-gather.9.cloned.1.call-done = bf16[4096,768]{1,0:T(8,128)(2,1)} async-done(((bf16[512,768]{1,0:T(8,128)(2,1)}), bf16[4096,768]{1,0:T(8,128)(2,1)}) %all-gather.9.cloned.1.call-update) | async-done | bytes 6291472 | tf_op jit(solution)/shard_map/all_gather | solution.py:70
  181.4 7.5 %convolution_convert_fusion.1 = bf16[512,768]{1,0:T(8,128)(2,1)S(1)} fusion(bf16[512,4096]{1,0:T(8,128)(2,1)} %all-gather.7.cloned.1.call-done, bf16[4096,768]{1,0:T(8,128)(2,1)} %all-gather.9.cloned.1.call-done), kind=kOutput, calls=%fused_computation.51 | convolution fusion | flops 3221618688 | bytes 11272192 | tf_op jit(solution)/shard_map/dot_general | solution.py:84
  189.4 0.6 subtract_convert_fusion.1
  190.2 55.7 %while.10 = (s32[]{:T(128)}, bf16[4,128,512]{2,1,0:T(8,128)(2,1)S(1)}, s32[4]{0:T(128)S(1)}, s32[4]{0:T(128)S(1)}, s32[4,24]{1,0:T(4,128)}, /*index=5*/bf16[96,1...) while((s32[]{:T(128)}, ...), condition=%wide.region_6.7_spmd, body=%wide.region_1.6_spmd.sunk | while | flops 856837184 | bytes 25968264 | solution.py:119
  190.2 0.6 dynamic_slice.56
  192.7 0.6 dynamic_slice.57
  193.3 0.6 iota_compare_fusion.4
  194.5 0.7 fusion.54
  195.2 3.4 %gather_fusion = bf16[24,128,256]{2,1,0:T(8,128)(2,1)S(1)} fusion(bf16[96,128,256]{2,1,0:T(8,128)(2,1)} %get-tuple-element.196, s32[1024]{0:T(1024)S(1)} %pad_clamp_fusion.4), kind=kCustom, calls=%fused_computation.clone.1 | custom fusion | bytes 3145824 | tf_op jit(solution)/shard_map/while/body/eval_jaxpr/gather | solution.py:45
  198.7 1.0 bitcast_reduce_fusion.2
  199.9 1.7 fusion.56
  201.7 2.0 fusion.57
  204.1 0.6 dynamic_slice.56
  206.6 0.6 dynamic_slice.57
  208.4 0.7 fusion.54
  209.1 3.5 %gather_fusion = bf16[24,128,256]{2,1,0:T(8,128)(2,1)S(1)} fusion(bf16[96,128,256]{2,1,0:T(8,128)(2,1)} %get-tuple-element.196, s32[1024]{0:T(1024)S(1)} %pad_clamp_fusion.4), kind=kCustom, calls=%fused_computation.clone.1 | custom fusion | bytes 3145824 | tf_op jit(solution)/shard_map/while/body/eval_jaxpr/gather | solution.py:45
  212.6 1.0 bitcast_reduce_fusion.2
  213.9 1.7 fusion.56
  215.6 2.0 fusion.57
  218.0 0.6 dynamic_slice.56
  220.6 0.6 dynamic_slice.57
  222.4 0.7 fusion.54
  223.1 3.5 %gather_fusion = bf16[24,128,256]{2,1,0:T(8,128)(2,1)S(1)} fusion(bf16[96,128,256]{2,1,0:T(8,128)(2,1)} %get-tuple-element.196, s32[1024]{0:T(1024)S(1)} %pad_clamp_fusion.4), kind=kCustom, calls=%fused_computation.clone.1 | custom fusion | bytes 3145824 | tf_op jit(solution)/shard_map/while/body/eval_jaxpr/gather | solution.py:45
  226.6 1.0 bitcast_reduce_fusion.2
  227.8 1.7 fusion.56
  229.6 2.0 fusion.57
  232.0 0.6 dynamic_slice.56
  234.5 0.6 dynamic_slice.57
  236.3 0.7 fusion.54
  237.0 3.4 %gather_fusion = bf16[24,128,256]{2,1,0:T(8,128)(2,1)S(1)} fusion(bf16[96,128,256]{2,1,0:T(8,128)(2,1)} %get-tuple-element.196, s32[1024]{0:T(1024)S(1)} %pad_clamp_fusion.4), kind=kCustom, calls=%fused_computation.clone.1 | custom fusion | bytes 3145824 | tf_op jit(solution)/shard_map/while/body/eval_jaxpr/gather | solution.py:45
  240.5 1.0 bitcast_reduce_fusion.2
  241.7 1.7 fusion.56
  243.5 2.0 fusion.57
  245.9 6.5 %convolution_convert_fusion = bf16[512,4096]{1,0:T(8,128)(2,1)} fusion(bf16[512,512]{1,0:T(8,128)(2,1)S(1)} %bitcast.107, bf16[512,4096]{0,1:T(8,128)(2,1)} %all-gather.11.cloned.1.call-done), kind=kOutput, calls=%fused_computation.45 | convolution fusion | flops 2149580800 | bytes 8912896 | tf_op jit(solution)/shard_map/dot_general | solution.py:121
  252.5 17.1 %reduce-scatter.3.cloned.1.call-done = bf16[256,4096]{1,0:T(8,128)(2,1)} async-done(((bf16[512,4096]{1,0:T(8,128)(2,1)}), bf16[256,4096]{1,0:T(8,128)(2,1)}) %reduce-scatter.3.cloned.1.call-update) | async-done | bytes 2097168 | tf_op jit(solution)/shard_map/reduce_scatter | solution.py:122
  269.6 0.8 copy.24
  270.5 41.1 %reduce-scatter.5.cloned.1.call-done = bf16[128,4096]{1,0:T(8,128)(2,1)} async-done(((bf16[256,4096]{1,0:T(8,128)(2,1)}), bf16[128,4096]{1,0:T(8,128)(2,1)}) %reduce-scatter.5.cloned.1.call-update) | async-done | bytes 1048592 | tf_op jit(solution)/shard_map/reduce_scatter | solution.py:123
  (76 shorter events, 5.5 us)
Async XLA Ops:
  7.2 67.9 %copy-start = (s32[256]{0:T(256)S(1)}, s32[256]{0:T(256)}, u32[]{:S(2)}) copy-start(s32[256]{0:T(256)} %param.15) | copy-start | bytes 3076
  7.2 25.5 %copy-start.2 = (bf16[64,768]{1,0:T(8,128)(2,1)S(1)}, bf16[64,768]{1,0:T(8,128)(2,1)}, u32[]{:S(2)}) copy-start(bf16[64,768]{1,0:T(8,128)(2,1)} %param.12) | copy-start | bytes 294916
  7.2 25.4 %all-gather.5.cloned.1.call-start = ((), (), s32[]{:S(2)}) async-start(), calls=%async_computation.2 | async-start | bytes 3145728 | tf_op jit(solution)/shard_map/all_gather | solution.py:81
  7.9 44.1 %copy-start.3 = (bf16[512,64]{0,1:T(8,128)(2,1)S(1)}, bf16[512,64]{0,1:T(8,128)(2,1)}, u32[]{:S(2)}) copy-start(bf16[512,64]{0,1:T(8,128)(2,1)} %param.13) | copy-start | bytes 196612
  12.0 63.7 %copy-start.1 = (s32[256]{0:T(256)S(1)}, s32[256]{0:T(256)}, u32[]{:S(2)}) copy-start(s32[256]{0:T(256)} %param.14) | copy-start | bytes 3076
  12.1 95.6 %all-gather.7.cloned.1.call-start = ((), (), s32[]{:S(2)}) async-start(), calls=%async_computation.3 | async-start | bytes 6291456 | tf_op jit(solution)/shard_map/all_gather | solution.py:80
  32.7 148.8 %all-gather.9.cloned.1.call-start = ((), (), s32[]{:S(2)}) async-start(), calls=%async_computation.4 | async-start | bytes 7077888 | tf_op jit(solution)/shard_map/all_gather | solution.py:70
  52.0 193.9 %all-gather.11.cloned.1.call-start = ((), (), s32[]{:S(2)}) async-start(), calls=%async_computation.5 | async-start | bytes 4718592 | tf_op jit(solution)/shard_map/all_gather | solution.py:70
  75.0 194.6 %reduce-scatter.3.cloned.1.call-start = ((), (), s32[]{:S(2)}) async-start(), calls=%async_computation.6 | async-start | bytes 6291456 | tf_op jit(solution)/shard_map/reduce_scatter | solution.py:122
  252.4 59.1 %reduce-scatter.5.cloned.1.call-start = ((), (), s32[]{:S(2)}) async-start(), calls=%async_computation.7 | async-start | bytes 3145728 | tf_op jit(solution)/shard_map/reduce_scatter | solution.py:123
Sparse Core Ops, SparseCore 0:
  12.2 20.4 all-gather.4
  34.4 73.1 all-gather.6
  109.4 71.9 all-gather.8
  183.1 53.3 all-gather.10
  252.6 16.9 reduce-scatter.2
  272.5 38.9 reduce-scatter.4
where the time goes:
time: 319 us; the launch traced here: 318 us
  waiting for transfers between devices  184 us (58%)
  blocking collectives  42.2 us (13%)
  matrix products  26.6 us (8%)
  local copies, waits for them, and re-layouts  21.4 us (7%)
  other arithmetic  19.2 us (6%)
  between operations  14.3 us (4%)
  loops' own time  10.8 us (3%)
    all_gather x2, waiting for transfers between devices, staged_gather(): values = lax.all_gather(values, name, axis=axis, tiled=True)  73.9 us
    all_gather x4, blocking collectives, staged_gather(): values = lax.all_gather(values, name, axis=axis, tiled=True)  42.2 us
    reduce_scatter x1, waiting for transfers between devices, per_device(): attn_out = lax.psum_scatter(partial, 'yhi', scatter_dimension=0, tiled=True)  41.1 us
    all_gather x1, waiting for transfers between devices, per_device(): lax.all_gather(lax.all_gather(normed, 'core', axis=0, tiled=True), 'yhi',...  31.1 us
    all_gather x1, waiting for transfers between devices, per_device(): lax.all_gather(normed, 'core', axis=0, tiled=True)  20.5 us
    reduce_scatter x1, waiting for transfers between devices, per_device(): partial = lax.psum_scatter(partial, 'core', scatter_dimension=0, tiled=True)  17.1 us
    gather x4, local copies, waits for them, and re-layouts, padded_attention(): cache = pool[page_row].reshape(-1, 2 * HEAD)  13.8 us
    another operation x1, loops' own time, per_device(): contexts = lax.map(attend, order)  10.8 us
  transfers between devices with their start and end apart: 6, of which 5 were waited for; matrix products, arithmetic and copies ran while one was open for 18% of the time, Pallas kernels for 0%

commit v1 on v0

--- a/solution.py
+++ b/solution.py
@@ -78,7 +78,12 @@
         jnp.bfloat16
     )
     gathered = lax.all_gather(
-        lax.all_gather(normed, "core", axis=0, tiled=True), "yhi", axis=0, tiled=True
+        jnp.concatenate(
+            lax.all_to_all(jnp.stack([normed] * lax.axis_size("core")), "core", 0, 0), axis=0
+        ),
+        "yhi",
+        axis=0,
+        tiled=True,
     )
     tok_rows = gathered.shape[0]
     projected = jnp.dot(

time: 319 us -> 307 us (0.962)
  waiting for transfers between devices: 184 us -> 165 us
  blocking collectives: 42.2 us -> 50 us
    all_gather x2 -> x1, waiting for transfers between devices: 51.6 us -> 31.6 us  [per_device(): lax.all_gather(jnp.concatenate(lax.all_to_all(jnp.stack([normed] * lax.ax...]
    all_to_all x0 -> x1, blocking collectives: none -> 9.27 us  [per_device(): lax.all_to_all(jnp.stack([normed] * lax.axis_size('core')), 'core', 0, 0)]
  transfers between devices with their start and end apart: 6 -> 5, of which waited for: 5 -> 4; matrix products, arithmetic and copies ran while one was open for 18% -> 18% of each run, Pallas kernels for 0% -> 0%
where the time goes in v1:
time: 307 us
  waiting for transfers between devices  165 us (54%)
  blocking collectives  50 us (16%)
  matrix products  26.6 us (9%)
  local copies, waits for them, and re-layouts  21.5 us (7%)
  other arithmetic  18.7 us (6%)
  between operations  14 us (5%)
  loops' own time  10.8 us (4%)
    all_gather x2, waiting for transfers between devices, staged_gather(): values = lax.all_gather(values, name, axis=axis, tiled=True)  75 us
    reduce_scatter x1, waiting for transfers between devices, per_device(): attn_out = lax.psum_scatter(partial, 'yhi', scatter_dimension=0, tiled=True)  41 us
    all_gather x4, blocking collectives, staged_gather(): values = lax.all_gather(values, name, axis=axis, tiled=True)  40.7 us
    all_gather x1, waiting for transfers between devices, per_device(): lax.all_gather(jnp.concatenate(lax.all_to_all(jnp.stack([normed] * lax.ax...  31.6 us
    reduce_scatter x1, waiting for transfers between devices, per_device(): partial = lax.psum_scatter(partial, 'core', scatter_dimension=0, tiled=True)  17.2 us
    gather x4, local copies, waits for them, and re-layouts, padded_attention(): cache = pool[page_row].reshape(-1, 2 * HEAD)  13.8 us
    another operation x1, loops' own time, per_device(): contexts = lax.map(attend, order)  10.8 us
    all_to_all x1, blocking collectives, per_device(): lax.all_to_all(jnp.stack([normed] * lax.axis_size('core')), 'core', 0, 0)  9.27 us
  transfers between devices with their start and end apart: 5, of which 4 were waited for; matrix products, arithmetic and copies ran while one was open for 18% of the time, Pallas kernels for 0%

profile of v1, /device:TPU:1, one launch (start us, length us, event | category | flops | bytes accessed | tf_op | source)
XLA Modules:
  0.0 306.6 jit_solution(15636669793997522801)
XLA Ops:
  7.2 0.7 convert_element_type.48
  7.9 1.5 fusion.29
  9.5 1.6 fusion.32
  11.2 9.3 %all_to_all.5 = bf16[2,128,4096]{2,1,0:T(8,128)(2,1)} all-to-all(bf16[2,128,4096]{2,1,0:T(8,128)(2,1)S(1)} %pad_maximum_fusion), channel_id=1, replica_groups=mesh['z'=8,'ylo'=2,'x'=4,'yhi'=2,'core'=2] {'core'}, dimensions={0} | all-to-all | bytes 4194304 | tf_op jit(solution)/shard_map/all_to_all | solution.py:82
  20.6 9.6 %all_gather.22 = bf16[256,768]{1,0:T(8,128)(2,1)S(1)} all-gather(bf16[64,768]{1,0:T(8,128)(2,1)S(1)} %copy-done.2), channel_id=1, replica_groups=mesh['z'=8,'ylo'=2,'x'=4,'yhi'=2,'core'=2] {'x'}, dimensions={0}, use_global_device_ids=true | all-gather | bytes 491520 | tf_op jit(solution)/shard_map/all_gather | solution.py:70
  30.2 7.8 %all_gather.23 = bf16[512,768]{1,0:T(8,128)(2,1)} all-gather(bf16[256,768]{1,0:T(8,128)(2,1)S(1)} %all_gather.22), channel_id=1, replica_groups=mesh['z'=8,'ylo'=2,'x'=4,'yhi'=2,'core'=2] {'ylo'}, dimensions={0}, use_global_device_ids=true | all-gather | bytes 1179648 | tf_op jit(solution)/shard_map/all_gather | solution.py:70
  38.1 10.6 %all_gather.25 = bf16[512,256]{0,1:T(8,128)(2,1)S(1)} all-gather(bf16[512,64]{0,1:T(8,128)(2,1)S(1)} %copy-done.3), channel_id=1, replica_groups=mesh['z'=8,'ylo'=2,'x'=4,'yhi'=2,'core'=2] {'x'}, dimensions={1}, use_global_device_ids=true | all-gather | bytes 327680 | tf_op jit(solution)/shard_map/all_gather | solution.py:70
  48.7 12.7 %all_gather.26 = bf16[512,512]{0,1:T(8,128)(2,1)} all-gather(bf16[512,256]{0,1:T(8,128)(2,1)S(1)} %all_gather.25), channel_id=1, replica_groups=mesh['z'=8,'ylo'=2,'x'=4,'yhi'=2,'core'=2] {'ylo'}, dimensions={1}, use_global_device_ids=true | all-gather | bytes 786432 | tf_op jit(solution)/shard_map/all_gather | solution.py:70
  61.6 0.6 gather_fusion.1
  62.2 0.6 gather_fusion.2
  62.9 31.6 %all-gather.4.cloned.1.call-done = bf16[512,4096]{1,0:T(8,128)(2,1)} async-done(((bf16[256,4096]{1,0:T(8,128)(2,1)}), bf16[512,4096]{1,0:T(8,128)(2,1)}) %all-gather.4.cloned.1.call-update) | async-done | bytes 4194320 | tf_op jit(solution)/shard_map/all_gather | solution.py:80
  94.5 75.0 %all-gather.6.cloned.1.call-done = bf16[4096,768]{1,0:T(8,128)(2,1)} async-done(((bf16[512,768]{1,0:T(8,128)(2,1)}), bf16[4096,768]{1,0:T(8,128)(2,1)}) %all-gather.6.cloned.1.call-update) | async-done | bytes 6291472 | tf_op jit(solution)/shard_map/all_gather | solution.py:70
  169.5 7.5 %convolution_convert_fusion.1 = bf16[512,768]{1,0:T(8,128)(2,1)S(1)} fusion(bf16[512,4096]{1,0:T(8,128)(2,1)} %all-gather.4.cloned.1.call-done, bf16[4096,768]{1,0:T(8,128)(2,1)} %all-gather.6.cloned.1.call-done), kind=kOutput, calls=%fused_computation.52 | convolution fusion | flops 3221618688 | bytes 11272192 | tf_op jit(solution)/shard_map/dot_general | solution.py:89
  178.2 56.1 %while.10 = (s32[]{:T(128)}, bf16[4,128,512]{2,1,0:T(8,128)(2,1)S(1)}, s32[4]{0:T(128)S(1)}, s32[4]{0:T(128)S(1)}, s32[4,24]{1,0:T(4,128)}, /*index=5*/bf16[96,1...) while((s32[]{:T(128)}, ...), condition=%wide.region_6.7_spmd, body=%wide.region_1.6_spmd.sunk | while | flops 856837184 | bytes 25968256 | solution.py:124
  178.2 0.6 dynamic_slice.56
  181.4 0.7 fusion.55
  182.1 3.4 %gather_fusion = bf16[24,128,256]{2,1,0:T(8,128)(2,1)S(1)} fusion(bf16[96,128,256]{2,1,0:T(8,128)(2,1)} %get-tuple-element.196, s32[1024]{0:T(1024)S(1)} %pad_clamp_fusion.4), kind=kCustom, calls=%fused_computation.clone.1 | custom fusion | bytes 3145824 | tf_op jit(solution)/shard_map/while/body/eval_jaxpr/gather | solution.py:45
  185.6 0.6 dynamic_slice.57
  186.2 0.7 iota_compare_fusion.4
  186.8 1.0 bitcast_reduce_fusion.2
  188.1 2.0 fusion.58
  190.1 1.7 fusion.57
  192.2 0.6 dynamic_slice.56
  195.4 0.7 fusion.55
  196.1 3.5 %gather_fusion = bf16[24,128,256]{2,1,0:T(8,128)(2,1)S(1)} fusion(bf16[96,128,256]{2,1,0:T(8,128)(2,1)} %get-tuple-element.196, s32[1024]{0:T(1024)S(1)} %pad_clamp_fusion.4), kind=kCustom, calls=%fused_computation.clone.1 | custom fusion | bytes 3145824 | tf_op jit(solution)/shard_map/while/body/eval_jaxpr/gather | solution.py:45
  199.6 0.6 dynamic_slice.57
  200.2 0.7 iota_compare_fusion.4
  200.9 1.0 bitcast_reduce_fusion.2
  202.2 2.0 fusion.58
  204.2 1.7 fusion.57
  206.3 0.6 dynamic_slice.56
  209.5 0.7 fusion.55
  210.2 3.5 %gather_fusion = bf16[24,128,256]{2,1,0:T(8,128)(2,1)S(1)} fusion(bf16[96,128,256]{2,1,0:T(8,128)(2,1)} %get-tuple-element.196, s32[1024]{0:T(1024)S(1)} %pad_clamp_fusion.4), kind=kCustom, calls=%fused_computation.clone.1 | custom fusion | bytes 3145824 | tf_op jit(solution)/shard_map/while/body/eval_jaxpr/gather | solution.py:45
  214.3 0.7 iota_compare_fusion.4
  214.9 1.0 bitcast_reduce_fusion.2
  216.3 2.0 fusion.58
  218.3 1.7 fusion.57
  223.6 0.7 fusion.55
  224.3 3.4 %gather_fusion = bf16[24,128,256]{2,1,0:T(8,128)(2,1)S(1)} fusion(bf16[96,128,256]{2,1,0:T(8,128)(2,1)} %get-tuple-element.196, s32[1024]{0:T(1024)S(1)} %pad_clamp_fusion.4), kind=kCustom, calls=%fused_computation.clone.1 | custom fusion | bytes 3145824 | tf_op jit(solution)/shard_map/while/body/eval_jaxpr/gather | solution.py:45
  227.7 0.6 dynamic_slice.57
  228.3 0.7 iota_compare_fusion.4
  228.9 1.0 bitcast_reduce_fusion.2
  230.3 2.0 fusion.58
  232.3 1.7 fusion.57
  234.4 6.5 %convolution_convert_fusion = bf16[512,4096]{1,0:T(8,128)(2,1)} fusion(bf16[512,512]{1,0:T(8,128)(2,1)S(1)} %bitcast.111, bf16[512,4096]{0,1:T(8,128)(2,1)} %all-gather.8.cloned.1.call-done), kind=kOutput, calls=%fused_computation.45 | convolution fusion | flops 2149580800 | bytes 8912896 | tf_op jit(solution)/shard_map/dot_general | solution.py:126
  241.0 17.2 %reduce-scatter.3.cloned.1.call-done = bf16[256,4096]{1,0:T(8,128)(2,1)} async-done(((bf16[512,4096]{1,0:T(8,128)(2,1)}), bf16[256,4096]{1,0:T(8,128)(2,1)}) %reduce-scatter.3.cloned.1.call-update) | async-done | bytes 2097168 | tf_op jit(solution)/shard_map/reduce_scatter | solution.py:127
  258.2 0.8 copy.24
  259.0 41.0 %reduce-scatter.5.cloned.1.call-done = bf16[128,4096]{1,0:T(8,128)(2,1)} async-done(((bf16[256,4096]{1,0:T(8,128)(2,1)}), bf16[128,4096]{1,0:T(8,128)(2,1)}) %reduce-scatter.5.cloned.1.call-update) | async-done | bytes 1048592 | tf_op jit(solution)/shard_map/reduce_scatter | solution.py:128
  (75 shorter events, 5.7 us)
Async XLA Ops:
  7.2 54.4 %copy-start = (s32[256]{0:T(256)S(1)}, s32[256]{0:T(256)}, u32[]{:S(2)}) copy-start(s32[256]{0:T(256)} %param.15) | copy-start | bytes 3076
  7.2 87.3 %all-gather.4.cloned.1.call-start = ((), (), s32[]{:S(2)}) async-start(), calls=%async_computation.3 | async-start | bytes 6291456 | tf_op jit(solution)/shard_map/all_gather | solution.py:80
  11.0 9.6 %copy-start.2 = (bf16[64,768]{1,0:T(8,128)(2,1)S(1)}, bf16[64,768]{1,0:T(8,128)(2,1)}, u32[]{:S(2)}) copy-start(bf16[64,768]{1,0:T(8,128)(2,1)} %param.12) | copy-start | bytes 294916
  11.2 26.9 %copy-start.3 = (bf16[512,64]{0,1:T(8,128)(2,1)S(1)}, bf16[512,64]{0,1:T(8,128)(2,1)}, u32[]{:S(2)}) copy-start(bf16[512,64]{0,1:T(8,128)(2,1)} %param.13) | copy-start | bytes 196612
  20.5 41.7 %copy-start.1 = (s32[256]{0:T(256)S(1)}, s32[256]{0:T(256)}, u32[]{:S(2)}) copy-start(s32[256]{0:T(256)} %param.14) | copy-start | bytes 3076
  20.5 149.0 %all-gather.6.cloned.1.call-start = ((), (), s32[]{:S(2)}) async-start(), calls=%async_computation.4 | async-start | bytes 7077888 | tf_op jit(solution)/shard_map/all_gather | solution.py:70
  38.1 196.3 %all-gather.8.cloned.1.call-start = ((), (), s32[]{:S(2)}) async-start(), calls=%async_computation.5 | async-start | bytes 4718592 | tf_op jit(solution)/shard_map/all_gather | solution.py:70
  61.4 196.7 %reduce-scatter.3.cloned.1.call-start = ((), (), s32[]{:S(2)}) async-start(), calls=%async_computation.6 | async-start | bytes 6291456 | tf_op jit(solution)/shard_map/reduce_scatter | solution.py:127
  240.9 59.2 %reduce-scatter.5.cloned.1.call-start = ((), (), s32[]{:S(2)}) async-start(), calls=%async_computation.7 | async-start | bytes 3145728 | tf_op jit(solution)/shard_map/reduce_scatter | solution.py:128
Sparse Core Ops, SparseCore 0:
  20.6 73.8 all-gather.3
  96.3 73.1 all-gather.5
  171.3 53.3 all-gather.7
  241.1 17.0 reduce-scatter.2
  261.1 38.9 reduce-scatter.4
